TPU v7x, 512 devices: a whole 4x8x8 slice. The times are simulated.
512 devices in a mesh: req: 64 (over x, y, core), head: 8 (over z).
Axes of the slice: x: 4, y: 8, z: 8, core: 2. Of those that a mesh axis runs over, the one named last changes fastest.
Arguments:
- queries: bfloat16 [2, 64, 128, 576], P(None, 'req', 'head'), may hold values from -100 to 100
- prompt_cache: bfloat16 [32768, 576], P('req'), may hold values from -10 to 10
- suffix_cache: bfloat16 [64, 8, 64, 576], P('req'), may hold values from -14 to 14
- new_latent: bfloat16 [2, 64, 576], P(None, 'req'), may hold values from -16 to 16
- suffix_len: int32 [64], P('req'), may hold values from 1 to 512, 16640 in all
- parent: int32 [64], P('req'), may hold values from 0 to 63
- fork_pages: int32 [64, 2], P('req'), may hold values from 0 to 7
Outputs:
- attended: bfloat16 [2, 64, 128, 512], P(None, 'req', 'head')
Inputs may be any that keep to these rules, and one draw needn't show every extreme that they name: `suffix_len`: every beam has at least one valid own token.
All inputs are finite; a program needn't handle non-finite values. No bound on the sum of `suffix_len` on one device may be relied on, other than what follows from the above.
Results may differ from a plain program's by a relative error of at most 0.008.
Values may be sent and summed in bfloat16 or wider, within the bound.
No kernel may reach another device: no remote copies, remote signals or barrier semaphores. Data moves between devices by JAX's collectives and lax.ppermute only.
A program may use at most 64 MiB of HBM per device.

v0:
```python
import math
import jax
import jax.numpy as jnp
from jax import lax
from jax.sharding import PartitionSpec as P

DL = 512
score_scale = 192.0 ** (-0.5)
neg_large = -1e30


def prompt_block(rows, keys):
    scores = (
        lax.dot_general(rows, keys, (((1,), (1,)), ((), ())), preferred_element_type=jnp.float32)
        * score_scale
    )
    top = jnp.max(scores, axis=-1)
    weights = jnp.exp(scores - top[:, None])
    total = jnp.sum(weights, axis=-1)
    summed = jnp.dot(weights.astype(jnp.bfloat16), keys[:, :DL], preferred_element_type=jnp.float32)
    return (top, total, (summed / total[:, None]).astype(jnp.bfloat16))


def masked_partial(queries, keys, valid):
    scores = (
        jnp.einsum("sbhk,btk->sbht", queries, keys, preferred_element_type=jnp.float32)
        * score_scale
    )
    scores = jnp.where(valid, scores, neg_large)
    top = jnp.max(scores, axis=-1)
    weights = jnp.where(valid, jnp.exp(scores - top[..., None]), 0.0)
    total = jnp.sum(weights, axis=-1)
    summed = jnp.einsum(
        "sbht,btd->sbhd",
        weights.astype(jnp.bfloat16),
        keys[..., :DL],
        preferred_element_type=jnp.float32,
    )
    return (top, total, summed)


def finish_fork(total, summed):
    return (summed / jnp.maximum(total, 1.0)[..., None]).astype(jnp.bfloat16)


def combine_parts(top_pr, total_pr, out_pr, top_fr, total_fr, out_fr, top_l, total_l, summed_l):
    peak = jnp.maximum(jnp.maximum(jnp.max(top_pr, axis=1), jnp.max(top_fr, axis=1)), top_l)
    weight_p = total_pr * jnp.exp(top_pr - peak[:, None])
    weight_f = total_fr * jnp.exp(top_fr - peak[:, None])
    weight_l = jnp.exp(top_l - peak)
    denom = jnp.sum(weight_p, axis=1) + jnp.sum(weight_f, axis=1) + total_l * weight_l
    numer = (
        jnp.sum(weight_p[..., None] * out_pr, axis=1)
        + jnp.sum(weight_f[..., None] * out_fr, axis=1)
        + weight_l[..., None] * summed_l
    )
    return numer / denom[..., None]


def on_device(queries, prompt_cache, suffix_cache, new_latent, suffix_len, parent, fork_pages):
    steps_n, beam_dev, head_dev, width = queries.shape
    pages_n, page_len = (suffix_cache.shape[1], suffix_cache.shape[2])
    forks_n = fork_pages.shape[1]
    req_n = lax.axis_size("req")
    first_beam = lax.axis_index("req") * beam_dev
    every_query = lax.all_gather(queries, "req", axis=1, tiled=True)
    all_parent, all_pages, all_len = (
        lax.all_gather(parent, "req", axis=0, tiled=True),
        lax.all_gather(fork_pages, "req", axis=0, tiled=True),
        lax.all_gather(suffix_len, "req", axis=0, tiled=True),
    )
    beams_n = every_query.shape[1]
    rows_n = steps_n * beams_n * head_dev
    block = math.gcd(rows_n, 512)
    blocks = every_query.reshape(rows_n // block, block, width)
    top_p, total_p, out_p = lax.map(lambda rows: prompt_block(rows, prompt_cache), blocks)
    top_p = top_p.reshape(steps_n, beams_n, head_dev)
    total_p = total_p.reshape(steps_n, beams_n, head_dev)
    out_p = out_p.reshape(steps_n, beams_n, head_dev, DL)
    local_parent = all_parent - first_beam
    owned = (local_parent >= 0) & (local_parent < beam_dev)
    source_beam = jnp.clip(local_parent, 0, beam_dev - 1)
    picked = suffix_cache[source_beam[:, None], all_pages]
    offsets = jnp.arange(page_len, dtype=jnp.int32)
    own_keys = jnp.concatenate(
        [suffix_cache.reshape(beam_dev, pages_n * page_len, width), jnp.swapaxes(new_latent, 0, 1)],
        axis=1,
    )
    old_valid = jnp.arange(pages_n * page_len, dtype=jnp.int32)[None, :] < suffix_len[:, None]
    new_valid = (
        jnp.arange(steps_n, dtype=jnp.int32)[None, :]
        <= jnp.arange(steps_n, dtype=jnp.int32)[:, None]
    )
    own_valid = jnp.concatenate(
        [
            jnp.broadcast_to(old_valid[None], (steps_n, beam_dev, pages_n * page_len)),
            new_valid[:, None, :],
        ],
        axis=2,
    )[:, :, None, :]
    top_l, total_l, summed_l = masked_partial(queries, own_keys, own_valid)
    outgoing = jnp.where(owned[:, None, None, None], picked, jnp.zeros_like(picked))
    arrived = lax.all_to_all(outgoing, "req", split_axis=0, concat_axis=0, tiled=True)
    tiles = jnp.sum(arrived.reshape(req_n, beam_dev, forks_n, page_len, width), axis=0)
    tiles = tiles.reshape(beam_dev, forks_n * page_len, width)
    positions = (fork_pages[:, :, None] * page_len + offsets[None, None, :]).reshape(beam_dev, -1)
    fork_valid = (positions < all_len[parent][:, None])[None, :, None, :]
    top_f, total_f, summed_f = masked_partial(queries, tiles, fork_valid)
    out_f = finish_fork(total_f, summed_f).astype(jnp.float32)
    out_pr, top_pr, total_pr = (
        lax.all_to_all(
            out_p.astype(jnp.float32), "req", split_axis=1, concat_axis=1, tiled=True
        ).astype(out_p.dtype),
        lax.all_to_all(top_p, "req", split_axis=1, concat_axis=1, tiled=True),
        lax.all_to_all(total_p, "req", split_axis=1, concat_axis=1, tiled=True),
    )
    top_pr = top_pr.reshape(steps_n, req_n, beam_dev, head_dev)
    total_pr = total_pr.reshape(steps_n, req_n, beam_dev, head_dev)
    out_pr = out_pr.astype(jnp.float32).reshape(steps_n, req_n, beam_dev, head_dev, DL)
    result = combine_parts(
        top_pr,
        total_pr,
        out_pr,
        top_f[:, None],
        total_f[:, None],
        out_f[:, None],
        top_l,
        total_l,
        summed_l,
    )
    return result.astype(jnp.bfloat16)


def solution(mesh):
    placed = (
        P(None, "req", "head", None),
        P("req", None),
        P("req", None, None, None),
        P(None, "req", None),
        P("req"),
        P("req"),
        P("req", None),
    )
    return jax.shard_map(
        on_device,
        mesh=mesh,
        in_specs=placed,
        out_specs=P(None, "req", "head", None),
        check_vma=False,
    )
```

profile of v0, /device:TPU:1, one launch (start us, length us, event | category | flops | bytes accessed | tf_op | source)
XLA Modules:
  0.0 454.0 jit_solution(4871701999400987592)
XLA Ops:
  6.5 0.7 all-gather.3.cloned.1.call-update
  8.6 39.9 %all-gather = s32[64,1,2]{2,1,0:T(1,128)S(1)} all-gather(s32[1,1,2]{2,1,0:T(1,128)} %bitcast.151), channel_id=1, replica_groups=mesh['req'=64,'head'=8] {'req'}, dimensions={0}, use_global_device_ids=true | all-gather | bytes 520 | tf_op jit(solution)/shard_map/all_gather | solution.py:69
  48.5 0.1 copy.24
  48.5 1.3 dynamic-slice.3
  49.9 0.7 dynamic-update-slice.2
  50.6 0.7 dynamic-update-slice.1
  51.4 13.4 %all-reduce.2 = (s32[64]{0:T(128)S(1)}, s32[64]{0:T(128)S(1)}) all-reduce(s32[64]{0:T(128)S(1)} %dynamic-update-slice.2, s32[64]{0:T(128)S(1)} %dynamic-update-slice.1), channel_id=1, replica_groups=mesh['req'=64,'head'=8] {'req'}, use_global_device_ids=true, to_apply=%add.1 | all-reduce | flops 128 | bytes 1024
  64.8 34.7 %all-gather.3.cloned.1.call-done = bf16[2,64,16,576]{3,2,1,0:T(8,128)(2,1)} async-done(((bf16[2,1,16,576]{3,2,1,0:T(8,128)(2,1)}), bf16[2,64,16,576]{3,2,1,0:T(8,128)(2,1)}) %all-gather.3.cloned.1.call-update) | async-done | bytes 2359312 | tf_op jit(solution)/shard_map/all_gather | solution.py:66
  99.5 11.2 %while.15 = (s32[]{:T(128)}, f32[4,512]{1,0:T(4,128)S(1)}, f32[4,512]{1,0:T(4,128)S(1)}, bf16[4,512,512]{2,1,0:T(8,128)(2,1)S(1)}, bf16[4,512,576]{2,1,0:T(8,128...) while((s32[]{:T(128)}, f32[4,512]{1,0:T(4,128)S(1)}, f32[4,512]{1,0:T(4,128)S(1)}, ...), condition=%wide.region_3.4_spmd, body=%wide.region_0.3_spmd.sunk | while | flops 572521472 | bytes 7817853 | solution.py:76
  99.5 2.0 fusion.73
  101.5 0.2 fusion.74
  101.7 0.5 fusion.75
  102.2 0.1 dynamic_update_slice.17
  102.3 0.1 dynamic_update_slice.16
  102.3 0.0 copy-start.1
  102.4 2.0 fusion.73
  104.3 0.2 fusion.74
  104.5 0.5 fusion.75
  105.0 0.1 dynamic_update_slice.17
  105.1 0.1 dynamic_update_slice.16
  105.2 0.0 copy-start.1
  105.2 2.0 fusion.73
  107.1 0.2 fusion.74
  107.3 0.5 fusion.75
  107.8 0.1 dynamic_update_slice.17
  107.9 0.1 dynamic_update_slice.16
  108.0 0.0 copy-start.1
  108.0 2.0 fusion.73
  109.9 0.2 fusion.74
  110.1 0.5 fusion.75
  110.7 0.1 dynamic_update_slice.17
  110.7 0.1 dynamic_update_slice.16
  110.8 0.1 reshape.289
  110.9 0.7 copy.23
  111.5 6.5 %all-to-all-start.1 = ((f32[2,64,16]{2,0,1:T(2,128)}), f32[2,64,16]{2,0,1:T(2,128)S(1)}, u32[]{:S(2)}, u32[]{:S(2)}) async-start(f32[2,64,16]{2,0,1:T(2,128)} %copy.23), calls=%async_computation.1 | async-start | bytes 131072 | tf_op jit(solution)/shard_map/all_to_all | solution.py:114
  118.1 0.1 copy.25
  118.2 0.1 reshape.321
  118.3 7.9 %gather_fusion = bf16[128,64,576]{2,1,0:T(8,128)(2,1)} fusion(bf16[1,8,64,576]{3,2,1,0:T(8,128)(2,1)S(1)} %copy-done, s32[128]{0:T(128)S(1)} %reshape.321), kind=kCustom, calls=%fused_computation | custom fusion | bytes 18875392 | tf_op jit(solution)/shard_map/gather | solution.py:83
  126.2 0.1 reshape.288
  126.3 0.7 copy.22
  127.0 0.9 all-to-all-done.1
  127.9 9.4 %all-to-all-start = ((f32[2,64,16]{2,0,1:T(2,128)}), f32[2,64,16]{2,0,1:T(2,128)S(1)}, u32[]{:S(2)}, u32[]{:S(2)}) async-start(f32[2,64,16]{2,0,1:T(2,128)} %copy.22), calls=%async_computation | async-start | bytes 131072 | tf_op jit(solution)/shard_map/all_to_all | solution.py:115
  137.3 10.0 %broadcast_select_fusion = bf16[64,2,64,576]{3,2,1,0:T(8,128)(2,1)} fusion(bf16[64,2,64,576]{3,2,1,0:T(8,128)(2,1)} %bitcast.144, pred[64]{0:T(512)(128)(4,1)S(1)} %compare_and_fusion), kind=kLoop, calls=%fused_computation.14 | loop fusion | flops 4718592 | bytes 18874432 | tf_op jit(solution)/shard_map/jit(_where)/select_n | solution.py:102
  147.3 0.0 all-to-all-done
  147.3 10.5 %all-to-all-start.2 = ((bf16[64,2,64,576]{3,2,1,0:T(8,128)(2,1)}), bf16[64,2,64,576]{3,2,1,0:T(8,128)(2,1)}, u32[]{:S(2)}, u32[]{:S(2)}) async-start(bf16[64,2,64,576]{3,2,1,0:T(8,128)(2,1)} %broadcast_select_fusion), calls=%async_computation.2 | async-start | bytes 20971520 | tf_op jit(solution)/shard_map/all_to_all | solution.py:103
  157.8 1.5 copy.27
  159.3 229.2 %all-to-all-done.2 = bf16[64,2,64,576]{3,2,1,0:T(8,128)(2,1)} async-done(((bf16[64,2,64,576]{3,2,1,0:T(8,128)(2,1)}), bf16[64,2,64,576]{3,2,1,0:T(8,128)(2,1)}, u32[]{:S(2)}, u32[]{:S(2)}) %all-to-all-start.2) | async-done | bytes 9437216 | tf_op jit(solution)/shard_map/all_to_all | solution.py:103
  388.5 5.9 %all-to-all-start.3 = ((bf16[2,64,16,512]{3,2,0,1:T(8,128)(2,1)}), bf16[2,64,16,512]{3,2,0,1:T(8,128)(2,1)S(1)}, u32[]{:S(2)}, u32[]{:S(2)}) async-start(bf16[2,64,16,512]{3,2,0,1:T(8,128)(2,1)} %copy.27), calls=%async_computation.3 | async-start | bytes 4194304 | tf_op jit(solution)/shard_map/all_to_all | solution.py:111
  394.4 0.1 add.66
  394.5 0.1 add.67
  394.6 0.1 add.69
  394.7 0.6 dynamic-slice.2
  395.4 0.4 fusion.60
  395.8 0.2 fusion.34
  396.0 0.7 add_compare_fusion
  396.6 0.1 reduce_max.40
  396.7 5.8 %reduce_sum.67 = bf16[2,64,576]{2,1,0:T(8,128)(2,1)S(1)} reduce(bf16[64,2,64,576]{3,2,1,0:T(8,128)(2,1)} %all-to-all-done.2, bf16[]{:T(256)} %constant.15.clone.1), dimensions={0}, to_apply=%region_5.6 | reduce | flops 4644864 | bytes 9584642 | tf_op jit(solution)/shard_map/reduce_sum | solution.py:104
  402.6 0.2 fusion.61
  402.8 0.2 fusion.44
  403.0 0.1 fusion.58
  403.1 42.5 %all-to-all-done.3 = bf16[2,64,16,512]{3,2,0,1:T(8,128)(2,1)S(1)} async-done(((bf16[2,64,16,512]{3,2,0,1:T(8,128)(2,1)}), bf16[2,64,16,512]{3,2,0,1:T(8,128)(2,1)S(1)}, u32[]{:S(2)}, u32[]{:S(2)}) %all-to-all-start.3) | async-done | bytes 2097184 | tf_op jit(solution)/shard_map/all_to_all | solution.py:111
  445.6 0.5 multiply_reduce_fusion
  446.1 0.2 fusion.24
  446.3 0.9 fusion.18
  (30 shorter events, 0.1 us)
Async XLA Ops:
  6.5 93.0 %all-gather.3.cloned.1.call-start = ((), (), s32[]{:S(2)}) async-start(), calls=%async_computation.4 | async-start | bytes 2662400 | tf_op jit(solution)/shard_map/all_gather | solution.py:66
  99.5 18.8 %copy-start = (bf16[1,8,64,576]{3,2,1,0:T(8,128)(2,1)S(1)}, bf16[1,8,64,576]{3,2,1,0:T(8,128)(2,1)}, u32[]{:S(2)}) copy-start(bf16[1,8,64,576]{3,2,1,0:T(8,128)(2,1)} %param.11) | copy-start | bytes 1769476
  99.5 2.2 copy-start.1
  102.3 2.2 copy-start.1
  105.2 2.2 copy-start.1
  108.0 2.2 copy-start.1
  111.5 16.4 %all-to-all-start.1 = ((f32[2,64,16]{2,0,1:T(2,128)}), f32[2,64,16]{2,0,1:T(2,128)S(1)}, u32[]{:S(2)}, u32[]{:S(2)}) async-start(f32[2,64,16]{2,0,1:T(2,128)} %copy.23), calls=%async_computation.1 | async-start | bytes 131072 | tf_op jit(solution)/shard_map/all_to_all | solution.py:114
  127.9 19.4 %all-to-all-start = ((f32[2,64,16]{2,0,1:T(2,128)}), f32[2,64,16]{2,0,1:T(2,128)S(1)}, u32[]{:S(2)}, u32[]{:S(2)}) async-start(f32[2,64,16]{2,0,1:T(2,128)} %copy.22), calls=%async_computation | async-start | bytes 131072 | tf_op jit(solution)/shard_map/all_to_all | solution.py:115
  147.3 241.2 %all-to-all-start.2 = ((bf16[64,2,64,576]{3,2,1,0:T(8,128)(2,1)}), bf16[64,2,64,576]{3,2,1,0:T(8,128)(2,1)}, u32[]{:S(2)}, u32[]{:S(2)}) async-start(bf16[64,2,64,576]{3,2,1,0:T(8,128)(2,1)} %broadcast_select_fusion), calls=%async_computation.2 | async-start | bytes 20971520 | tf_op jit(solution)/shard_map/all_to_all | solution.py:103
  159.3 235.1 %copy-start.3 = (s32[1,2]{1,0:T(1,128)S(1)}, s32[1,2]{1,0:T(1,128)}, u32[]{:S(2)}) copy-start(s32[1,2]{1,0:T(1,128)} %param.15) | copy-start | bytes 28
  159.3 236.0 %copy-start.2 = (bf16[2,1,16,576]{3,2,1,0:T(8,128)(2,1)S(1)}, bf16[2,1,16,576]{3,2,1,0:T(8,128)(2,1)}, u32[]{:S(2)}) copy-start(bf16[2,1,16,576]{3,2,1,0:T(8,128)(2,1)} %param.9) | copy-start | bytes 110596
  159.3 236.0 %copy-start.4 = (bf16[2,1,576]{2,0,1:T(2,128)(2,1)S(1)}, bf16[2,1,576]{2,0,1:T(2,128)(2,1)}, u32[]{:S(2)}) copy-start(bf16[2,1,576]{2,0,1:T(2,128)(2,1)} %param.12) | copy-start | bytes 6916
  388.5 57.1 %all-to-all-start.3 = ((bf16[2,64,16,512]{3,2,0,1:T(8,128)(2,1)}), bf16[2,64,16,512]{3,2,0,1:T(8,128)(2,1)S(1)}, u32[]{:S(2)}, u32[]{:S(2)}) async-start(bf16[2,64,16,512]{3,2,0,1:T(8,128)(2,1)} %copy.27), calls=%async_computation.3 | async-start | bytes 4194304 | tf_op jit(solution)/shard_map/all_to_all | solution.py:111
Sparse Core Ops, SparseCore 0:
  10.6 88.8 all-gather.2
where the time goes:
time: 455 us; the launch traced here: 454 us
  waiting for transfers between devices  308 us (68%)
  blocking collectives  53.3 us (12%)
  starting transfers between devices  32.3 us (7%)
  other arithmetic  18.3 us (4%)
  local copies, waits for them, and re-layouts  15.4 us (3%)
  between operations  14.9 us (3%)
  matrix products  11.6 us (3%)
    all_to_all x1, waiting for transfers between devices, on_device(): lax.all_to_all(outgoing, 'req', split_axis=0, concat_axis=0, tiled=True)  229 us
    all_to_all x1, waiting for transfers between devices, on_device(): lax.all_to_all(out_p.astype(jnp.float32), 'req', split_axis=1, concat_axi...  42.5 us
    all_gather x1, blocking collectives, on_device(): lax.all_gather(fork_pages, 'req', axis=0, tiled=True)  39.9 us
    all_gather x1, waiting for transfers between devices, on_device(): every_query = lax.all_gather(queries, 'req', axis=1, tiled=True)  34.7 us
    unnamed x1, blocking collectives  13.4 us
    all_to_all x1, starting transfers between devices, on_device(): lax.all_to_all(outgoing, 'req', split_axis=0, concat_axis=0, tiled=True)  10.5 us
    select_n x1, other arithmetic, on_device(): jnp.where(owned[:, None, None, None], picked, jnp.zeros_like(picked))  9.98 us
    all_to_all x1, starting transfers between devices, on_device(): lax.all_to_all(total_p, 'req', split_axis=1, concat_axis=1, tiled=True)  9.44 us
  transfers between devices with their start and end apart: 5, of which 4 were waited for; matrix products, arithmetic and copies ran while one was open for 7% of the time, Pallas kernels for 0%

commit v1 on v0

--- a/solution.py
+++ b/solution.py
@@ -63,7 +63,9 @@
     forks_n = fork_pages.shape[1]
     req_n = lax.axis_size("req")
     first_beam = lax.axis_index("req") * beam_dev
-    every_query = lax.all_gather(queries, "req", axis=1, tiled=True)
+    every_query = jnp.concatenate(
+        lax.all_to_all(jnp.stack([queries] * lax.axis_size("req")), "req", 0, 0), axis=1
+    )
     all_parent, all_pages, all_len = (
         lax.all_gather(parent, "req", axis=0, tiled=True),
         lax.all_gather(fork_pages, "req", axis=0, tiled=True),

time: 455 us -> 476 us (1.046)
  blocking collectives: 53.3 us -> 102 us
  waiting for transfers between devices: 308 us -> 273 us
  starting transfers between devices: 32.3 us -> 47.4 us
  between operations: 14.9 us -> 1.56 us
  local copies, waits for them, and re-layouts: 15.4 us -> 23 us
    all_gather x1, blocking collectives: 39.9 us -> 87.6 us  [on_device(): lax.all_gather(fork_pages, 'req', axis=0, tiled=True)]
    all_gather x1 -> x0, waiting for transfers between devices: 34.7 us -> none  [on_device(): every_query = lax.all_gather(queries, 'req', axis=1, tiled=True)]
    all_to_all x0 -> x1, starting transfers between devices: none -> 11.7 us  [on_device(): lax.all_to_all(jnp.stack([queries] * lax.axis_size('req')), 'req', 0, 0)]
  transfers between devices with their start and end apart: 5 -> 5, of which waited for: 4 -> 3; matrix products, arithmetic and copies ran while one was open for 7% -> 7% of each run, Pallas kernels for 0% -> 0%
where the time goes in v1:
time: 476 us
  waiting for transfers between devices  273 us (57%)
  blocking collectives  102 us (21%)
  starting transfers between devices  47.4 us (10%)
  local copies, waits for them, and re-layouts  23 us (5%)
  other arithmetic  18.3 us (4%)
  matrix products  10.7 us (2%)
    all_to_all x1, waiting for transfers between devices, on_device(): lax.all_to_all(outgoing, 'req', split_axis=0, concat_axis=0, tiled=True)  229 us
    all_gather x1, blocking collectives, on_device(): lax.all_gather(fork_pages, 'req', axis=0, tiled=True)  87.6 us
    all_to_all x1, waiting for transfers between devices, on_device(): lax.all_to_all(out_p.astype(jnp.float32), 'req', split_axis=1, concat_axi...  42.5 us
    unnamed x1, blocking collectives  14.5 us
    all_to_all x1, starting transfers between devices, on_device(): lax.all_to_all(jnp.stack([queries] * lax.axis_size('req')), 'req', 0, 0)  11.7 us
    all_to_all x1, starting transfers between devices, on_device(): lax.all_to_all(outgoing, 'req', split_axis=0, concat_axis=0, tiled=True)  10.5 us
    select_n x1, other arithmetic, on_device(): jnp.where(owned[:, None, None, None], picked, jnp.zeros_like(picked))  9.98 us
    all_to_all x1, starting transfers between devices, on_device(): lax.all_to_all(top_p, 'req', split_axis=1, concat_axis=1, tiled=True)  9.84 us
  transfers between devices with their start and end apart: 5, of which 3 were waited for; matrix products, arithmetic and copies ran while one was open for 7% of the time, Pallas kernels for 0%

profile of v1, /device:TPU:1, one launch (start us, length us, event | category | flops | bytes accessed | tf_op | source)
XLA Modules:
  0.0 475.6 jit_solution(11226184820793423930)
XLA Ops:
  0.0 2.5 stack.2
  2.5 11.7 %all-to-all-start = ((bf16[64,2,1,16,576]{4,3,1,2,0:T(8,128)(2,1)}), bf16[64,2,1,16,576]{4,3,1,2,0:T(8,128)(2,1)S(1)}, u32[]{:S(2)}, u32[]{:S(2)}) async-start(bf16[64,2,1,16,576]{4,3,1,2,0:T(8,128)(2,1)} %stack.2), calls=%async_computation | async-start | bytes 5242880 | tf_op jit(solution)/shard_map/all_to_all | solution.py:67
  15.6 87.6 %all-gather = s32[64,1,2]{2,1,0:T(1,128)S(1)} all-gather(s32[1,1,2]{2,1,0:T(1,128)S(1)} %bitcast.154), channel_id=1, replica_groups=mesh['req'=64,'head'=8] {'req'}, dimensions={0}, use_global_device_ids=true | all-gather | bytes 520 | tf_op jit(solution)/shard_map/all_gather | solution.py:71
  103.2 0.1 copy.25
  103.3 1.3 dynamic-slice.3
  104.5 0.7 dynamic-update-slice.2
  105.3 0.7 dynamic-update-slice.1
  106.0 14.5 %all-reduce.2 = (s32[64]{0:T(128)S(1)}, s32[64]{0:T(128)S(1)}) all-reduce(s32[64]{0:T(128)S(1)} %dynamic-update-slice.2, s32[64]{0:T(128)S(1)} %dynamic-update-slice.1), channel_id=1, replica_groups=mesh['req'=64,'head'=8] {'req'}, use_global_device_ids=true, to_apply=%add.1 | all-reduce | flops 128 | bytes 1024
  120.5 0.0 all-to-all-done
  120.5 1.5 copy-done.2
  122.0 3.6 copy.22
  125.7 10.3 %while.15 = (s32[]{:T(128)}, f32[4,512]{1,0:T(4,128)S(1)}, f32[4,512]{1,0:T(4,128)S(1)}, bf16[4,512,512]{2,1,0:T(8,128)(2,1)S(1)}, bf16[4,512,576]{2,1,0:T(8,128...) while((s32[]{:T(128)}, f32[4,512]{1,0:T(4,128)S(1)}, f32[4,512]{1,0:T(4,128)S(1)}, ...), condition=%wide.region_3.4_spmd, body=%wide.region_0.3_spmd.sunk | while | flops 572521472 | bytes 5458529 | solution.py:78
  125.7 1.8 fusion.73
  127.5 0.2 fusion.74
  127.7 0.5 fusion.75
  128.2 0.1 dynamic_update_slice.17
  128.2 0.1 dynamic_update_slice.16
  128.3 1.7 fusion.73
  130.0 0.2 fusion.74
  130.2 0.5 fusion.75
  130.7 0.1 dynamic_update_slice.17
  130.8 0.1 dynamic_update_slice.16
  130.8 1.7 fusion.73
  132.6 0.2 fusion.74
  132.8 0.5 fusion.75
  133.3 0.1 dynamic_update_slice.17
  133.3 0.1 dynamic_update_slice.16
  133.4 1.7 fusion.73
  135.1 0.2 fusion.74
  135.3 0.5 fusion.75
  135.8 0.1 dynamic_update_slice.17
  135.9 0.1 dynamic_update_slice.16
  135.9 0.1 reshape.290
  136.0 0.7 copy.24
  136.7 9.8 %all-to-all-start.2 = ((f32[2,64,16]{2,0,1:T(2,128)}), f32[2,64,16]{2,0,1:T(2,128)S(1)}, u32[]{:S(2)}, u32[]{:S(2)}) async-start(f32[2,64,16]{2,0,1:T(2,128)} %copy.24), calls=%async_computation.2 | async-start | bytes 131072 | tf_op jit(solution)/shard_map/all_to_all | solution.py:116
  146.6 0.1 copy.26
  146.7 0.1 reshape.321
  146.8 7.9 %gather_fusion = bf16[128,64,576]{2,1,0:T(8,128)(2,1)} fusion(bf16[1,8,64,576]{3,2,1,0:T(8,128)(2,1)S(1)} %copy-done, s32[128]{0:T(128)S(1)} %reshape.321), kind=kCustom, calls=%fused_computation | custom fusion | bytes 18875392 | tf_op jit(solution)/shard_map/gather | solution.py:85
  154.7 0.1 reshape.289
  154.8 0.7 copy.23
  155.5 0.9 all-to-all-done.2
  156.4 9.4 %all-to-all-start.1 = ((f32[2,64,16]{2,0,1:T(2,128)}), f32[2,64,16]{2,0,1:T(2,128)S(1)}, u32[]{:S(2)}, u32[]{:S(2)}) async-start(f32[2,64,16]{2,0,1:T(2,128)} %copy.23), calls=%async_computation.1 | async-start | bytes 131072 | tf_op jit(solution)/shard_map/all_to_all | solution.py:117
  165.8 10.0 %broadcast_select_fusion = bf16[64,2,64,576]{3,2,1,0:T(8,128)(2,1)} fusion(bf16[64,2,64,576]{3,2,1,0:T(8,128)(2,1)} %bitcast.145, pred[64]{0:T(512)(128)(4,1)S(1)} %compare_and_fusion), kind=kLoop, calls=%fused_computation.14 | loop fusion | flops 4718592 | bytes 18874432 | tf_op jit(solution)/shard_map/jit(_where)/select_n | solution.py:104
  175.8 0.0 all-to-all-done.1
  175.8 10.5 %all-to-all-start.3 = ((bf16[64,2,64,576]{3,2,1,0:T(8,128)(2,1)}), bf16[64,2,64,576]{3,2,1,0:T(8,128)(2,1)}, u32[]{:S(2)}, u32[]{:S(2)}) async-start(bf16[64,2,64,576]{3,2,1,0:T(8,128)(2,1)} %broadcast_select_fusion), calls=%async_computation.3 | async-start | bytes 20971520 | tf_op jit(solution)/shard_map/all_to_all | solution.py:105
  186.3 1.6 copy.28
  187.9 229.1 %all-to-all-done.3 = bf16[64,2,64,576]{3,2,1,0:T(8,128)(2,1)} async-done(((bf16[64,2,64,576]{3,2,1,0:T(8,128)(2,1)}), bf16[64,2,64,576]{3,2,1,0:T(8,128)(2,1)}, u32[]{:S(2)}, u32[]{:S(2)}) %all-to-all-start.3) | async-done | bytes 9437216 | tf_op jit(solution)/shard_map/all_to_all | solution.py:105
  417.0 5.9 %all-to-all-start.4 = ((bf16[2,64,16,512]{3,2,0,1:T(8,128)(2,1)}), bf16[2,64,16,512]{3,2,0,1:T(8,128)(2,1)S(1)}, u32[]{:S(2)}, u32[]{:S(2)}) async-start(bf16[2,64,16,512]{3,2,0,1:T(8,128)(2,1)} %copy.28), calls=%async_computation.4 | async-start | bytes 4194304 | tf_op jit(solution)/shard_map/all_to_all | solution.py:113
  422.9 0.1 add.66
  422.9 0.1 add.67
  423.0 0.1 add.69
  423.1 0.6 dynamic-slice.2
  423.8 0.4 fusion.60
  424.2 0.2 fusion.34
  424.4 0.7 add_compare_fusion
  425.1 0.1 reduce_max.40
  425.2 5.8 %reduce_sum.67 = bf16[2,64,576]{2,1,0:T(8,128)(2,1)S(1)} reduce(bf16[64,2,64,576]{3,2,1,0:T(8,128)(2,1)} %all-to-all-done.3, bf16[]{:T(256)} %constant.15.clone.1), dimensions={0}, to_apply=%region_5.6 | reduce | flops 4644864 | bytes 9584642 | tf_op jit(solution)/shard_map/reduce_sum | solution.py:106
  431.0 0.2 fusion.61
  431.3 0.2 fusion.42
  431.5 0.1 fusion.58
  431.6 42.5 %all-to-all-done.4 = bf16[2,64,16,512]{3,2,0,1:T(8,128)(2,1)S(1)} async-done(((bf16[2,64,16,512]{3,2,0,1:T(8,128)(2,1)}), bf16[2,64,16,512]{3,2,0,1:T(8,128)(2,1)S(1)}, u32[]{:S(2)}, u32[]{:S(2)}) %all-to-all-start.4) | async-done | bytes 2097184 | tf_op jit(solution)/shard_map/all_to_all | solution.py:113
  474.1 0.5 multiply_reduce_fusion
  474.5 0.2 fusion.24
  474.7 0.9 fusion.18
  (29 shorter events, 0.1 us)
Async XLA Ops:
  2.5 13.1 %copy-start.5 = (s32[1,2]{1,0:T(1,128)S(1)}, s32[1,2]{1,0:T(1,128)}, u32[]{:S(2)}) copy-start(s32[1,2]{1,0:T(1,128)} %param.15) | copy-start | bytes 28
  2.5 118.0 %all-to-all-start = ((bf16[64,2,1,16,576]{4,3,1,2,0:T(8,128)(2,1)}), bf16[64,2,1,16,576]{4,3,1,2,0:T(8,128)(2,1)S(1)}, u32[]{:S(2)}, u32[]{:S(2)}) async-start(bf16[64,2,1,16,576]{4,3,1,2,0:T(8,128)(2,1)} %stack.2), calls=%async_computation | async-start | bytes 5242880 | tf_op jit(solution)/shard_map/all_to_all | solution.py:67
  120.5 1.5 copy-start.2
  122.0 3.6 copy-start.1
  122.0 3.6 copy-start.3
  125.7 21.2 %copy-start = (bf16[1,8,64,576]{3,2,1,0:T(8,128)(2,1)S(1)}, bf16[1,8,64,576]{3,2,1,0:T(8,128)(2,1)}, u32[]{:S(2)}) copy-start(bf16[1,8,64,576]{3,2,1,0:T(8,128)(2,1)} %param.11) | copy-start | bytes 1769476
  136.7 19.7 %all-to-all-start.2 = ((f32[2,64,16]{2,0,1:T(2,128)}), f32[2,64,16]{2,0,1:T(2,128)S(1)}, u32[]{:S(2)}, u32[]{:S(2)}) async-start(f32[2,64,16]{2,0,1:T(2,128)} %copy.24), calls=%async_computation.2 | async-start | bytes 131072 | tf_op jit(solution)/shard_map/all_to_all | solution.py:116
  156.4 19.4 %all-to-all-start.1 = ((f32[2,64,16]{2,0,1:T(2,128)}), f32[2,64,16]{2,0,1:T(2,128)S(1)}, u32[]{:S(2)}, u32[]{:S(2)}) async-start(f32[2,64,16]{2,0,1:T(2,128)} %copy.23), calls=%async_computation.1 | async-start | bytes 131072 | tf_op jit(solution)/shard_map/all_to_all | solution.py:117
  175.8 241.2 %all-to-all-start.3 = ((bf16[64,2,64,576]{3,2,1,0:T(8,128)(2,1)}), bf16[64,2,64,576]{3,2,1,0:T(8,128)(2,1)}, u32[]{:S(2)}, u32[]{:S(2)}) async-start(bf16[64,2,64,576]{3,2,1,0:T(8,128)(2,1)} %broadcast_select_fusion), calls=%async_computation.3 | async-start | bytes 20971520 | tf_op jit(solution)/shard_map/all_to_all | solution.py:105
  187.9 235.9 %copy-start.4 = (bf16[2,1,16,576]{3,2,1,0:T(8,128)(2,1)S(1)}, bf16[2,1,16,576]{3,2,1,0:T(8,128)(2,1)}, u32[]{:S(2)}) copy-start(bf16[2,1,16,576]{3,2,1,0:T(8,128)(2,1)} %param.9) | copy-start | bytes 110596
  187.9 236.0 %copy-start.6 = (bf16[2,1,576]{2,0,1:T(2,128)(2,1)S(1)}, bf16[2,1,576]{2,0,1:T(2,128)(2,1)}, u32[]{:S(2)}) copy-start(bf16[2,1,576]{2,0,1:T(2,128)(2,1)} %param.12) | copy-start | bytes 6916
  417.0 57.1 %all-to-all-start.4 = ((bf16[2,64,16,512]{3,2,0,1:T(8,128)(2,1)}), bf16[2,64,16,512]{3,2,0,1:T(8,128)(2,1)S(1)}, u32[]{:S(2)}, u32[]{:S(2)}) async-start(bf16[2,64,16,512]{3,2,0,1:T(8,128)(2,1)} %copy.28), calls=%async_computation.4 | async-start | bytes 4194304 | tf_op jit(solution)/shard_map/all_to_all | solution.py:113
